TPU v7x, 32 devices: a whole 2x2x4 slice. The times are simulated.
32 devices in a mesh: groups: 2 (over y), tiles: 4 (over z), sections: 2 (over x), chan: 2 (over core).
Axes of the slice: x: 2, y: 2, z: 4, core: 2. Of those that a mesh axis runs over, the one named last changes fastest.
Arguments:
- features: bfloat16 [8, 16, 64, 1024], P('groups', ('tiles', 'chan')), parts along dimension 0, may hold values from -6 to 6
- tissue: int32 [8, 16, 64], P('groups', ('tiles', 'chan')), parts along dimension 0, may hold values from 0 to 1, as said below
- row_label: int32 [8, 16], P('groups', ('tiles', 'chan')), parts along dimension 0, may hold values from 0 to 1
- prototypes: bfloat16 [2, 1024], replicated, may hold values from -5 to 5
- reduce_weight: bfloat16 [2, 1024, 256], P('sections', 'chan'), may hold values from -0.1875 to 0.1875
- spatial_weight: bfloat16 [2, 3, 3, 256, 256], P('sections', None, None, None, 'chan'), may hold values from -0.125 to 0.125
- expand_weight: bfloat16 [2, 256, 1024], P('sections', None, 'chan'), may hold values from -0.375 to 0.375
- norm_gain: float32 [2, 2, 256], P('sections'), may hold values from 0.25 to 1.75
- norm_bias: float32 [2, 2, 256], P('sections'), may hold values from -3 to 3
Outputs:
- grad_reduce: bfloat16 [4, 1024, 256], P(('groups', 'sections'), 'chan'), parts along dimension 0
- grad_spatial: bfloat16 [4, 3, 3, 256, 256], P(('groups', 'sections'), None, None, None, 'chan'), parts along dimension 0
- grad_expand: bfloat16 [4, 256, 1024], P(('groups', 'sections'), None, 'chan'), parts along dimension 0
- grad_gain: float32 [4, 2, 256], P(('groups', 'sections'), None, 'chan'), parts along dimension 0
- grad_bias: float32 [4, 2, 256], P(('groups', 'sections'), None, 'chan'), parts along dimension 0
There are 2 independent parts, one for each index of `groups`. A program takes and returns all parts, laid end to end along the dimension named above; an argument that names none is the same for every part. Nothing has to cross between parts.
Inputs may be any that keep to these rules, and one draw needn't show every extreme that they name: 1 marks a tissue cell, 0 background.
All inputs are finite; a program needn't handle non-finite values.
Results may differ from a plain program's by a relative error of at most 0.011.
Values may be sent and summed in bfloat16 or wider, within the bound.
No kernel may reach another device: no remote copies, remote signals or barrier semaphores. Data moves between devices by JAX's collectives and lax.ppermute only.
A program may use at most 128 MiB of HBM per device.

v0:
```python
import functools
import jax
import jax.numpy as jnp
from jax import lax
from jax.sharding import PartitionSpec as P

ROW_AXES = ("tiles", "chan")


def halo_rows(block):
    count = lax.axis_size(ROW_AXES)
    forward = [(i, i + 1) for i in range(count - 1)]
    backward = [(target, source) for source, target in forward]
    low = lax.ppermute(block[:, -1:], ROW_AXES, forward)
    high = lax.ppermute(block[:, :1], ROW_AXES, backward)
    return jnp.concatenate([low, block, high], axis=1)


def grid_taps(extended, height, breadth, mirrored):
    padded = jnp.pad(extended, ((0, 0), (0, 0), (1, 1), (0, 0)))
    tap_list = []
    for shift_row in range(3):
        for shift_col in range(3):
            if mirrored:
                start_row = 2 - shift_row
                start_col = 2 - shift_col
            else:
                start_row = shift_row
                start_col = shift_col
            tap_list.append(
                padded[:, start_row : start_row + height, start_col : start_col + breadth]
            )
    stacked = jnp.concatenate(tap_list, axis=3)
    return stacked.reshape(extended.shape[0] * height * breadth, stacked.shape[3])


def gather_blocks(half, chan_axis, chain, position):
    received = [
        lax.ppermute(half, "sections", [(i, (i + k) % chain) for i in range(chain)])
        for k in range(1, chain)
    ]
    stacked = jnp.stack([half] + received)
    if chan_axis is not None:
        stacked = lax.all_gather(stacked, "chan", axis=chan_axis + 1, tiled=True)
    return [
        lax.dynamic_index_in_dim(stacked, (position - b + chain) % chain, 0, keepdims=False)
        for b in range(chain)
    ]


def weight_partials(ops, cells, height, breadth):
    cur, h1e, h2, reduced, spatial_out, grad_block, masked_two, grad_two, masked_one, grad_one = ops
    full = cur.shape[-1]
    inner = h2.shape[-1]
    block_flat = grad_block.reshape(cells, full)
    two_flat = grad_two.reshape(cells, inner)
    one_flat = grad_one.reshape(cells, inner)
    reduce_term = jnp.dot(
        cur.reshape(cells, full).T, one_flat, preferred_element_type=jnp.float32
    ).astype(jnp.bfloat16)
    spatial_term = jnp.dot(
        grid_taps(h1e, height, breadth, False).T, two_flat, preferred_element_type=jnp.float32
    ).astype(jnp.bfloat16)
    expand_term = jnp.dot(
        h2.reshape(cells, inner).T, block_flat, preferred_element_type=jnp.float32
    ).astype(jnp.bfloat16)
    gain = jnp.stack(
        [
            jnp.sum(masked_one * reduced, axis=(0, 1, 2)),
            jnp.sum(masked_two * spatial_out, axis=(0, 1, 2)),
        ]
    )
    bias = jnp.stack([jnp.sum(masked_one, axis=(0, 1, 2)), jnp.sum(masked_two, axis=(0, 1, 2))])
    small = jnp.concatenate([gain, bias]).astype(jnp.bfloat16)
    return (
        reduce_term.reshape(2, full // 2, inner),
        spatial_term.reshape(9 * inner, 2, inner // 2).transpose(1, 0, 2),
        expand_term.reshape(inner, 2, full // 2).transpose(1, 0, 2),
        small.reshape(4, 2, inner // 2).transpose(1, 0, 2),
    )


def local(
    features,
    tissue,
    row_label,
    prototypes,
    reduce_weight,
    spatial_weight,
    expand_weight,
    norm_gain,
    norm_bias,
):
    regions, height, breadth, full_width = features.shape
    chain = lax.axis_size("sections")
    position = lax.axis_index("sections")
    chan_index = lax.axis_index("chan")
    reduce_all = gather_blocks(reduce_weight[0], 0, chain, position)
    spatial_all = gather_blocks(spatial_weight[0], 3, chain, position)
    expand_all = gather_blocks(expand_weight[0], 1, chain, position)
    gain_all = gather_blocks(norm_gain[0], None, chain, position)
    bias_all = gather_blocks(norm_bias[0], None, chain, position)
    inner_width = reduce_all[0].shape[1]
    tissue_mask = tissue.astype(jnp.float32)[:, :, :, None]
    cells = regions * height * breadth
    inner_shape = (regions, height, breadth, inner_width)
    outer_shape = (regions, height, breadth, full_width)
    current = features
    saved = []
    for b in range(chain):
        gain_pair, bias_pair = (gain_all[b], bias_all[b])
        reduced = jnp.dot(
            current.reshape(cells, full_width), reduce_all[b], preferred_element_type=jnp.float32
        ).reshape(inner_shape)
        pre_reduce = gain_pair[0] * reduced + bias_pair[0]
        hidden_one = jnp.maximum(pre_reduce, 0.0).astype(jnp.bfloat16)
        hidden_ext = halo_rows(hidden_one)
        spatial_out = jnp.dot(
            grid_taps(hidden_ext, height, breadth, False),
            spatial_all[b].reshape(9 * inner_width, inner_width),
            preferred_element_type=jnp.float32,
        ).reshape(inner_shape)
        pre_spatial = gain_pair[1] * spatial_out + bias_pair[1]
        hidden_two = jnp.maximum(pre_spatial, 0.0).astype(jnp.bfloat16)
        expanded = jnp.dot(
            hidden_two.reshape(cells, inner_width),
            expand_all[b],
            preferred_element_type=jnp.float32,
        ).reshape(outer_shape)
        block_out = (tissue_mask * jnp.maximum(current.astype(jnp.float32) + expanded, 0.0)).astype(
            jnp.bfloat16
        )
        saved.append(
            (
                current,
                hidden_ext,
                reduced,
                pre_reduce,
                spatial_out,
                pre_spatial,
                hidden_two,
                block_out,
            )
        )
        current = block_out
    classes = prototypes.shape[0]
    chosen = (row_label[:, :, None] == jnp.arange(classes, dtype=jnp.int32)).astype(jnp.float32)
    target_rows = jnp.einsum("mrk,kc->mrc", chosen, prototypes.astype(jnp.float32))
    total_cells = regions * height * lax.axis_size("tiles") * lax.axis_size("chan") * breadth
    upstream = (
        tissue_mask * (current.astype(jnp.float32) - target_rows[:, :, None, :]) / total_cells
    ).astype(jnp.bfloat16)
    block_ops = [None] * chain
    for b in reversed(range(chain)):
        (
            block_in,
            hidden_ext,
            reduced,
            pre_reduce,
            spatial_out,
            pre_spatial,
            hidden_two,
            block_out,
        ) = saved[b]
        needed = b >= position
        gain_pair = gain_all[b]

        def first_back(
            upstream=upstream,
            block_out=block_out,
            pre_spatial=pre_spatial,
            b=b,
            gain_pair=gain_pair,
        ):
            grad_block = jnp.where(block_out > 0, upstream, jnp.zeros_like(upstream))
            back_two = jnp.dot(
                grad_block.reshape(cells, full_width),
                expand_all[b].T,
                preferred_element_type=jnp.float32,
            ).reshape(inner_shape)
            masked_two = jnp.where(pre_spatial > 0, back_two, jnp.float32(0.0))
            grad_two = (masked_two * gain_pair[1]).astype(jnp.bfloat16)
            return (grad_block, masked_two, grad_two)

        def first_skip():
            return (
                jnp.zeros(outer_shape, jnp.bfloat16),
                jnp.zeros(inner_shape, jnp.float32),
                jnp.zeros(inner_shape, jnp.bfloat16),
            )

        grad_block, masked_two, grad_two = lax.cond(needed, first_back, first_skip)
        grad_ext = halo_rows(grad_two)

        def second_back(grad_ext=grad_ext, pre_reduce=pre_reduce, b=b, gain_pair=gain_pair):
            back_one = jnp.dot(
                grid_taps(grad_ext, height, breadth, True),
                jnp.transpose(spatial_all[b], (0, 1, 3, 2)).reshape(9 * inner_width, inner_width),
                preferred_element_type=jnp.float32,
            ).reshape(inner_shape)
            masked_one = jnp.where(pre_reduce > 0, back_one, jnp.float32(0.0))
            grad_one = (masked_one * gain_pair[0]).astype(jnp.bfloat16)
            return (masked_one, grad_one)

        def second_skip():
            return (jnp.zeros(inner_shape, jnp.float32), jnp.zeros(inner_shape, jnp.bfloat16))

        masked_one, grad_one = lax.cond(needed, second_back, second_skip)
        block_ops[b] = (
            block_in,
            hidden_ext,
            hidden_two,
            reduced,
            spatial_out,
            grad_block,
            masked_two,
            grad_two,
            masked_one,
            grad_one,
        )
        if b > 0:

            def pass_back(grad_block=grad_block, grad_one=grad_one, b=b):
                return (
                    grad_block.astype(jnp.float32)
                    + jnp.dot(
                        grad_one.reshape(cells, inner_width),
                        reduce_all[b].T,
                        preferred_element_type=jnp.float32,
                    ).reshape(outer_shape)
                ).astype(jnp.bfloat16)

            upstream = lax.cond(
                b > position, pass_back, lambda: jnp.zeros(outer_shape, jnp.bfloat16)
            )
    partials = lax.switch(
        position,
        [
            functools.partial(lambda k: weight_partials(block_ops[k], cells, height, breadth), k)
            for k in range(chain)
        ],
    )
    totals = []
    for piece in partials:
        mine = lax.dynamic_index_in_dim(piece, chan_index, 0, keepdims=False)
        theirs = lax.dynamic_index_in_dim(piece, 1 - chan_index, 0, keepdims=False)
        arrived = lax.ppermute(theirs, "chan", [(0, 1), (1, 0)])
        pair_sum = (mine.astype(jnp.float32) + arrived.astype(jnp.float32)).astype(jnp.bfloat16)
        totals.append(lax.psum(pair_sum, "tiles"))
    half_inner = inner_width // 2
    grad_reduce = totals[0][None]
    grad_spatial = totals[1].reshape(3, 3, inner_width, half_inner)[None]
    grad_expand = totals[2][None]
    small = totals[3].astype(jnp.float32)
    return (grad_reduce, grad_spatial, grad_expand, small[0:2][None], small[2:4][None])


def solution(mesh):
    placed = (
        P("groups", ("tiles", "chan"), None, None),
        P("groups", ("tiles", "chan"), None),
        P("groups", ("tiles", "chan")),
        P(),
        P("sections", "chan", None),
        P("sections", None, None, None, "chan"),
        P("sections", None, "chan"),
        P("sections", None, None),
        P("sections", None, None),
    )
    return jax.shard_map(
        local,
        mesh=mesh,
        in_specs=placed,
        out_specs=(
            P(("groups", "sections"), "chan", None),
            P(("groups", "sections"), None, None, None, "chan"),
            P(("groups", "sections"), None, "chan"),
            P(("groups", "sections"), None, "chan"),
            P(("groups", "sections"), None, "chan"),
        ),
        check_vma=False,
    )
```

profile of v0, /device:TPU:0, one launch (start us, length us, event | category | flops | bytes accessed | tf_op | source)
XLA Modules:
  0.0 206.3 jit_solution(13812828813498507578)
XLA Ops:
  7.2 3.0 %collective-permute-start.1 = (bf16[512,256]{1,0:T(8,128)(2,1)}, bf16[512,256]{1,0:T(8,128)(2,1)S(1)}, u32[]{:S(2)}, u32[]{:S(2)}) collective-permute-start(bf16[512,256]{1,0:T(8,128)(2,1)} %bitcast.257), channel_id=1, source_target_pairs={{0,2},{2,0},{1,3},{3,1},{4,6},{6,4},{5,7},{7,5},{8,10},{10,8},{9,1... | collective-permute-start | bytes 786440 | tf_op jit(solution)/shard_map/ppermute | solution.py:39
  10.3 6.5 %collective-permute-done.1 = bf16[512,256]{1,0:T(8,128)(2,1)S(1)} collective-permute-done((bf16[512,256]{1,0:T(8,128)(2,1)}, bf16[512,256]{1,0:T(8,128)(2,1)S(1)}, u32[]{:S(2)}, u32[]{:S(2)}) %collective-permute-start.1) | collective-permute-done | bytes 262176 | tf_op jit(solution)/shard_map/ppermute | solution.py:39
  22.0 12.8 %collective-permute-done.5 = bf16[3,3,256,128]{2,3,1,0:T(8,128)(2,1)S(1)} collective-permute-done((bf16[3,3,256,128]{2,3,1,0:T(8,128)(2,1)S(1)}, bf16[3,3,256,128]{2,3,1,0:T(8,128)(2,1)S(1)}, u32[]{:S(2)}, u32[]{:S(2)}) %collective-permute-start.5) | collective-permute-done | bytes 589856 | tf_op jit(solution)/shard_map/ppermute | solution.py:39
  47.4 2.8 %collective-permute-done.4 = bf16[4,1,64,256]{3,2,1,0:T(8,128)(2,1)S(1)} collective-permute-done((bf16[4,1,64,256]{3,2,1,0:T(8,128)(2,1)S(1)}, bf16[4,1,64,256]{3,2,1,0:T(8,128)(2,1)S(1)}, u32[]{:S(2)}, u32[]{:S(2)}) %collective-permute-start.4) | collective-permute-done | bytes 131104 | tf_op jit(solution)/shard_map/ppermute | solution.py:15
  57.3 3.0 %constant_dynamic-slice_fusion.6 = (bf16[1,3,3,256,256]{3,4,2,1,0:T(8,128)(2,1)}, bf16[1,3,3,256,256]{3,4,2,1,0:T(8,128)(2,1)S(1)}) fusion(bf16[2,3,3,256,256]{3,4,2,1,0:T(8,128)(2,1)} %all-gather.6.cloned.1.call-done, s32[]{:T(128)S(6)} %select_n.84, s32[]{:T(128)S(6)} %select_n.82), kind=kLoop, calls=%fused_computation.185 | loop fusion | bytes 4718600 | tf_op jit(solution)/shard_map/jit(dynamic_index_in_dim)/dynamic_slice | solution.py:46
  61.8 3.6 %maximum_convert_fusion.2 = (bf16[4,2,64,256]{3,2,1,0:T(8,128)(2,1)}, f32[4,2,64,256]{3,2,1,0:T(8,128)S(1)}, f32[4,2,64,256]{3,2,1,0:T(8,128)}) fusion(f32[256]{0:T(256)S(1)} %bitcast.263, f32[256]{0:T(256)S(1)} %bitcast.264, bf16[4,2,64,2304]{3,2,1,0:T(8,128)(2,1)} %fusion.50, bf16[2304,256,1,1]{1,0,3,2:T(8,128)(2,1)} %bitcast.246), kind=kOutput, calls=%fused_computation.127 | convolution fusion | flops 604504064 | bytes 4851712 | tf_op jit(solution)/shard_map/dot_general | solution.py:118
  65.5 2.1 %multiply_convert_fusion.6 = bf16[4,2,64,1024]{3,2,1,0:T(8,128)(2,1)S(1)} fusion(bf16[4,2,64,1024]{3,2,1,0:T(8,128)(2,1)} %param.21, f32[4,2,64]{2,1,0:T(2,128)S(1)} %convert_element_type.145, bf16[2,256,1024]{2,1,0:T(8,128)(2,1)} %all-gather.8.cloned.1.call-done, s32[]{:T(128)S(6)} %select_n.82, f32[4,2,64,256]{3,2,1,0:T(8,128)S(1)} %get-tuple-element.187), kind=kOutput, calls=%fused_computation.102 | convolution fusion | flops 271319040 | bytes 3147780 | tf_op jit(solution)/shard_map/dot_general | solution.py:125
  68.9 5.3 %collective-permute-start.7 = (bf16[4,1,64,256]{3,2,1,0:T(8,128)(2,1)S(1)}, bf16[4,1,64,256]{3,2,1,0:T(8,128)(2,1)S(1)}, u32[]{:S(2)}, u32[]{:S(2)}) collective-permute-start(bf16[4,1,64,256]{3,2,1,0:T(8,128)(2,1)S(1)} %get-tuple-element.212), channel_id=1, source_target_pairs={{0,1},{1,4},{4,5},{5,8},{8,9},{9,12},{12,13},{2,3},{3,6},{6,7},{7,... | collective-permute-start | bytes 393224 | tf_op jit(solution)/shard_map/ppermute | solution.py:14
  76.6 2.4 %copy.28 = bf16[1,3,3,256,256]{4,3,2,1,0:T(8,128)(2,1)} copy(bf16[1,3,3,256,256]{3,4,2,1,0:T(8,128)(2,1)} %get-tuple-element.204) | data formatting | bytes 2359296 | tf_op jit(solution)/shard_map/jit(dynamic_index_in_dim)/dynamic_slice | solution.py:46
  85.7 3.6 %conditional.6 = (bf16[4,2,64,1024]{3,2,1,0:T(8,128)(2,1)}, f32[4,2,64,256]{3,2,1,0:T(8,128)}, bf16[4,2,64,256]{3,2,1,0:T(8,128)(2,1)S(1)}) conditional(s32[]{:T(128)} %convert_element_type.151, () %tuple.57, (bf16[4,2,64,1024]{3,2,1,0:T(8,128)(2,1)S(1)}, bf16[4,2,64,1024]{3,2,1,0:T(8,128)(2,1)S(1)}, f32[4,2,64,256]{3,2,1,0:T(8,128)S(1)}, ...), branch_computations={%region_0.1_spmd, %region_1.2_spmd} | conditional | flops 270008320 | bytes 6032408 | solution.py:192
  86.7 2.6 %multiply_convert_fusion = (bf16[4,2,64,256]{3,2,1,0:T(8,128)(2,1)S(1)}, f32[4,2,64,256]{3,2,1,0:T(8,128)}) fusion(f32[256]{0:T(256)S(1)} %bitcast.271, bf16[4,2,64,1024]{3,2,1,0:T(8,128)(2,1)} %compare_select_fusion, bf16[256,1024]{1,0:T(8,128)(2,1)S(1)} %get-tuple-element.90, f32[4,2,64,256]{3,2,1,0:T(8,128)S(1)} %get-tuple-element.89), kind=kOutput, calls=%fused_computation.3 | convolution fusion | flops 268959744 | bytes 2884608 | tf_op jit(solution)/shard_map/cond/branch_1_fun/dot_general | solution.py:176
  90.0 3.7 %collective-permute-start.9 = (bf16[4,1,64,256]{3,2,1,0:T(8,128)(2,1)}, bf16[4,1,64,256]{3,2,1,0:T(8,128)(2,1)}, u32[]{:S(2)}, u32[]{:S(2)}) collective-permute-start(bf16[4,1,64,256]{3,2,1,0:T(8,128)(2,1)} %get-tuple-element.210), channel_id=1, source_target_pairs={{0,1},{1,4},{4,5},{5,8},{8,9},{9,12},{12,13},{2,3},{3,6},{6,7},{7,... | collective-permute-start | bytes 393224 | tf_op jit(solution)/shard_map/ppermute | solution.py:14
  98.2 3.1 %conditional.7 = (f32[4,2,64,256]{3,2,1,0:T(8,128)}, bf16[4,2,64,256]{3,2,1,0:T(8,128)(2,1)S(1)}) conditional(s32[]{:T(128)} %convert_element_type.151, () %tuple.59, (f32[4,2,64,256]{3,2,1,0:T(8,128)}, bf16[4,4,64,256]{3,2,1,0:T(8,128)(2,1)S(1)}, bf16[1,3,3,256,256]{3,4,2,1,0:T(8,128)(2,1)}, f32[2,256]{1,0:T(2,128)S(1)}) %tuple.139), branch_computations={%region_2.3_spmd, %region_3.4_spmd} | conditional | flops 604504064 | bytes 17960008 | solution.py:208
  101.9 2.9 %conditional.8 = (bf16[4,2,64,1024]{3,2,1,0:T(8,128)(2,1)}) conditional(s32[]{:T(128)} %convert_element_type.150, () %tuple.56, (bf16[4,2,64,1024]{3,2,1,0:T(8,128)(2,1)}, bf16[4,2,64,256]{3,2,1,0:T(8,128)(2,1)S(1)}, bf16[1024,256]{1,0:T(8,128)(2,1)}) %tuple.61), branch_computations={%region_4.5_spmd, %region_5.6_spmd} | conditional | flops 270008320 | bytes 2883592 | solution.py:233
  101.9 2.9 %add_convert_fusion = bf16[4,2,64,1024]{3,2,1,0:T(8,128)(2,1)} fusion(bf16[4,2,64,1024]{3,2,1,0:T(8,128)(2,1)} %get-tuple-element.96, bf16[4,2,64,256]{3,2,1,0:T(8,128)(2,1)S(1)} %get-tuple-element.97, bf16[1024,256]{1,0:T(8,128)(2,1)} %get-tuple-element.98), kind=kOutput, calls=%fused_computation.21 | convolution fusion | flops 270008320 | bytes 2883584 | tf_op jit(solution)/shard_map/cond/branch_1_fun/dot_general | solution.py:226
  104.8 4.2 %conditional.9 = (bf16[4,2,64,1024]{3,2,1,0:T(8,128)(2,1)}, f32[4,2,64,256]{3,2,1,0:T(8,128)S(1)}, bf16[4,2,64,256]{3,2,1,0:T(8,128)(2,1)S(1)}) conditional(s32[]{:T(128)} %convert_element_type.144, () %tuple.55, (bf16[4,2,64,1024]{3,2,1,0:T(8,128)(2,1)S(1)}, bf16[4,2,64,1024]{3,2,1,0:T(8,128)(2,1)}, f32[4,2,64,256]{3,2,1,0:T(8,128)}, ...), branch_computations={%region_6.7_spmd, %region_7.8_spmd} | conditional | flops 270008320 | bytes 10226768 | solution.py:192
  104.8 2.5 %compare_select_fusion.1 = bf16[4,2,64,1024]{3,2,1,0:T(8,128)(2,1)} fusion(bf16[4,2,64,1024]{3,2,1,0:T(8,128)(2,1)} %get-tuple-element.100, bf16[4,2,64,1024]{3,2,1,0:T(8,128)(2,1)S(1)} %get-tuple-element.99), kind=kLoop, calls=%fused_computation.23 | loop fusion | flops 1048576 | bytes 3145728 | tf_op jit(solution)/shard_map/cond/branch_1_fun/jit(_where)/select_n | solution.py:175
  110.4 6.1 %collective-permute-start.11 = (bf16[4,1,64,256]{3,2,1,0:T(8,128)(2,1)}, bf16[4,1,64,256]{3,2,1,0:T(8,128)(2,1)}, u32[]{:S(2)}, u32[]{:S(2)}) collective-permute-start(bf16[4,1,64,256]{3,2,1,0:T(8,128)(2,1)} %get-tuple-element.208), channel_id=1, source_target_pairs={{0,1},{1,4},{4,5},{5,8},{8,9},{9,12},{12,13},{2,3},{3,6},{6,7},{7,... | collective-permute-start | bytes 393224 | tf_op jit(solution)/shard_map/ppermute | solution.py:14
  120.9 2.5 %conditional.10 = (f32[4,2,64,256]{3,2,1,0:T(8,128)S(1)}, bf16[4,2,64,256]{3,2,1,0:T(8,128)(2,1)S(1)}) conditional(s32[]{:T(128)} %convert_element_type.144, () %tuple.54, (f32[4,2,64,256]{3,2,1,0:T(8,128)}, bf16[4,4,64,256]{3,2,1,0:T(8,128)(2,1)S(1)}, bf16[1,3,3,256,256]{3,4,2,1,0:T(8,128)(2,1)}, f32[2,256]{1,0:T(2,128)S(1)}) %tuple.137), branch_computations={%region_8.9_spmd, %region_9.10_spmd} | conditional | flops 604504064 | bytes 17960008 | solution.py:208
  123.4 8.0 %conditional.11 = (bf16[2,512,256]{2,1,0:T(8,128)(2,1)}, bf16[2,2304,128]{1,2,0:T(8,128)(2,1)S(1)}, bf16[2,4,128]{2,0,1:T(2,128)(2,1)S(1)}, bf16[2,256,512]{2,1,0:T(8,128)(2,1)S(1)}, bf16[2,4,128]{2,1,0:T(4,128)(2,1)S(1)}) conditional(s32[]{:T(128)} %clamp.3, (bf16[4,2,64,1024]{3,2,1,0:T(8,128)(2,1)}, bf16[4,2,64,256]{3,2,1,0:T(8,128)(2,1)S(1)}, ...), branch_computations={%region_10.15_spmd, %region_15.20_spmd} | conditional | flops 1142753280 | bytes 23226548 | solution.py:236
  125.0 2.5 %fusion.16 = bf16[1024,256]{1,0:T(8,128)(2,1)} fusion(bf16[4,2,64,1024]{3,2,1,0:T(8,128)(2,1)} %get-tuple-element.108, bf16[4,2,64,256]{3,2,1,0:T(8,128)(2,1)S(1)} %get-tuple-element.109), kind=kOutput, calls=%fused_computation.48 | convolution fusion | flops 268697600 | bytes 1835008 | tf_op jit(solution)/shard_map/cond/branch_0_fun/dot_general | solution.py:58
  131.5 2.5 %collective-permute-start.15 = (bf16[256,512]{1,0:T(8,128)(2,1)S(1)}, bf16[256,512]{1,0:T(8,128)(2,1)}, u32[]{:S(2)}, u32[]{:S(2)}) collective-permute-start(bf16[256,512]{1,0:T(8,128)(2,1)S(1)} %dynamic-slice_bitcast_fusion.4), channel_id=1, source_target_pairs={{0,1},{1,0},{2,3},{3,2},{4,5},{5,4},{6,7},{7,6},{8,9},{9,8},{10,11... | collective-permute-start | bytes 786440 | tf_op jit(solution)/shard_map/ppermute | solution.py:247
  142.3 10.8 %psum.31 = bf16[4,128]{1,0:T(4,128)(2,1)S(1)} all-reduce(bf16[4,128]{1,0:T(4,128)(2,1)S(1)} %fusion.73), channel_id=1, replica_groups=mesh['groups'=2,'tiles'=4,'sections'=2,'chan'=2] {'tiles'}, use_global_device_ids=true, to_apply=%region_23.24 | all-reduce | flops 512 | bytes 2048 | tf_op jit(solution)/shard_map/psum | solution.py:249
  153.6 40.9 %all-reduce.9.cloned.1.call-done = (bf16[1,512,256]{2,1,0:T(8,128)(2,1)}, bf16[1,3,3,256,128]{4,3,2,1,0:T(8,128)(2,1)}, bf16[1,256,512]{2,1,0:T(8,128)(2,1)}) async-done(((bf16[1,512,256]{2,1,0:T(8,128)(2,1)}, bf16[1,3,3,256,128]{4,3,2,1,0:T(8,128)(2,1)}, bf16[1,256,512]{2,1,0:T(8,128)(2,1)}), (bf16[1,512,256]{2,1,0:T(8,128)(2,1)}, bf16[1,3,3,256,128]{4,3,2,1,0:T(8,128)(2,1)}, ...) | async-done | bytes 1114128 | tf_op jit(solution)/shard_map/psum | solution.py:249
  (208 shorter events, 75.7 us)
Async XLA Ops:
  7.2 32.5 %copy-start = (bf16[2,1024]{1,0:T(2,128)(2,1)S(1)}, bf16[2,1024]{1,0:T(2,128)(2,1)}, u32[]{:S(2)}) copy-start(bf16[2,1024]{1,0:T(2,128)(2,1)} %param.24) | copy-start | bytes 12292
  7.2 34.0 %all-gather.4.cloned.1.call-start = ((), (), s32[]{:S(2)}) async-start(), calls=%async_computation | async-start | bytes 1572864 | tf_op jit(solution)/shard_map/all_gather | solution.py:44
  7.2 9.5 %collective-permute-start.1 = (bf16[512,256]{1,0:T(8,128)(2,1)}, bf16[512,256]{1,0:T(8,128)(2,1)S(1)}, u32[]{:S(2)}, u32[]{:S(2)}) collective-permute-start(bf16[512,256]{1,0:T(8,128)(2,1)} %bitcast.257), channel_id=1, source_target_pairs={{0,2},{2,0},{1,3},{3,1},{4,6},{6,4},{5,7},{7,5},{8,10},{10,8},{9,1... | collective-permute-start | bytes 786440 | tf_op jit(solution)/shard_map/ppermute | solution.py:39
  18.7 22.5 %copy-start.18 = (bf16[4,2,64,1024]{3,2,1,0:T(8,128)(2,1)S(1)}, bf16[4,2,64,1024]{3,2,1,0:T(8,128)(2,1)}, u32[]{:S(2)}) copy-start(bf16[4,2,64,1024]{3,2,1,0:T(8,128)(2,1)} %param.21) | copy-start | bytes 3145732
  18.7 38.7 %all-gather.6.cloned.1.call-start = ((), (), s32[]{:S(2)}) async-start(), calls=%async_computation.1 | async-start | bytes 3538944 | tf_op jit(solution)/shard_map/all_gather | solution.py:44
  20.2 14.6 %collective-permute-start.5 = (bf16[3,3,256,128]{2,3,1,0:T(8,128)(2,1)S(1)}, bf16[3,3,256,128]{2,3,1,0:T(8,128)(2,1)S(1)}, u32[]{:S(2)}, u32[]{:S(2)}) collective-permute-start(bf16[3,3,256,128]{2,3,1,0:T(8,128)(2,1)S(1)} %bitcast.248), channel_id=1, source_target_pairs={{0,2},{2,0},{1,3},{3,1},{4,6},{6,4},{5,7},{7,5},{8,10},{10,8},{9,1... | collective-permute-start | bytes 1769480 | tf_op jit(solution)/shard_map/ppermute | solution.py:39
  35.9 29.6 %all-gather.8.cloned.1.call-start = ((), (), s32[]{:S(2)}) async-start(), calls=%async_computation.2 | async-start | bytes 1572864 | tf_op jit(solution)/shard_map/all_gather | solution.py:44
  36.0 4.5 %collective-permute-start.2 = (f32[2,256]{1,0:T(2,128)S(1)}, f32[2,256]{1,0:T(2,128)S(1)}, u32[]{:S(2)}, u32[]{:S(2)}) collective-permute-start(f32[2,256]{1,0:T(2,128)S(1)} %bitcast.284), channel_id=1, source_target_pairs={{0,2},{2,0},{1,3},{3,1},{4,6},{6,4},{5,7},{7,5},{8,10},{10,8},{9,1... | collective-permute-start | bytes 6152 | tf_op jit(solution)/shard_map/ppermute | solution.py:39
  37.5 3.6 %collective-permute-start = (f32[2,256]{1,0:T(2,128)S(1)}, f32[2,256]{1,0:T(2,128)S(1)}, u32[]{:S(2)}, u32[]{:S(2)}) collective-permute-start(f32[2,256]{1,0:T(2,128)S(1)} %bitcast.283), channel_id=1, source_target_pairs={{0,2},{2,0},{1,3},{3,1},{4,6},{6,4},{5,7},{7,5},{8,10},{10,8},{9,1... | collective-permute-start | bytes 6152 | tf_op jit(solution)/shard_map/ppermute | solution.py:39
  38.1 8.4 %collective-permute-start.6 = (bf16[256,512]{1,0:T(8,128)(2,1)S(1)}, bf16[256,512]{1,0:T(8,128)(2,1)S(1)}, u32[]{:S(2)}, u32[]{:S(2)}) collective-permute-start(bf16[256,512]{1,0:T(8,128)(2,1)S(1)} %bitcast.258), channel_id=1, source_target_pairs={{0,2},{2,0},{1,3},{3,1},{4,6},{6,4},{5,7},{7,5},{8,10},{10,8},{9,1... | collective-permute-start | bytes 786440 | tf_op jit(solution)/shard_map/ppermute | solution.py:39
  40.4 25.1 %copy-start.32 = (f32[4,2,64]{2,1,0:T(2,128)}, f32[4,2,64]{2,1,0:T(2,128)S(1)}, u32[]{:S(2)}) copy-start(f32[4,2,64]{2,1,0:T(2,128)S(1)} %convert_element_type.145) | copy-start | bytes 6148
  43.9 3.6 %collective-permute-start.3 = (bf16[4,1,64,256]{3,2,1,0:T(8,128)(2,1)S(1)}, bf16[4,1,64,256]{3,2,1,0:T(8,128)(2,1)S(1)}, u32[]{:S(2)}, u32[]{:S(2)}) collective-permute-start(bf16[4,1,64,256]{3,2,1,0:T(8,128)(2,1)S(1)} %get-tuple-element.214), channel_id=1, source_target_pairs={{0,1},{1,4},{4,5},{5,8},{8,9},{9,12},{12,13},{2,3},{3,6},{6,7},{7,... | collective-permute-start | bytes 393224 | tf_op jit(solution)/shard_map/ppermute | solution.py:14
  45.2 5.0 %collective-permute-start.4 = (bf16[4,1,64,256]{3,2,1,0:T(8,128)(2,1)S(1)}, bf16[4,1,64,256]{3,2,1,0:T(8,128)(2,1)S(1)}, u32[]{:S(2)}, u32[]{:S(2)}) collective-permute-start(bf16[4,1,64,256]{3,2,1,0:T(8,128)(2,1)S(1)} %get-tuple-element.215), channel_id=1, source_target_pairs={{1,0},{4,1},{5,4},{8,5},{9,8},{12,9},{13,12},{3,2},{6,3},{7,6},{10... | collective-permute-start | bytes 393224 | tf_op jit(solution)/shard_map/ppermute | solution.py:15
  47.4 147.1 %all-reduce.9.cloned.1.call-start = ((), (), s32[]{:S(2)}) async-start(), calls=%async_computation.3 | async-start | bytes 2228224 | tf_op jit(solution)/shard_map/psum | solution.py:249
  68.9 10.1 %collective-permute-start.7 = (bf16[4,1,64,256]{3,2,1,0:T(8,128)(2,1)S(1)}, bf16[4,1,64,256]{3,2,1,0:T(8,128)(2,1)S(1)}, u32[]{:S(2)}, u32[]{:S(2)}) collective-permute-start(bf16[4,1,64,256]{3,2,1,0:T(8,128)(2,1)S(1)} %get-tuple-element.212), channel_id=1, source_target_pairs={{0,1},{1,4},{4,5},{5,8},{8,9},{9,12},{12,13},{2,3},{3,6},{6,7},{7,... | collective-permute-start | bytes 393224 | tf_op jit(solution)/shard_map/ppermute | solution.py:14
  74.2 5.4 %collective-permute-start.8 = (bf16[4,1,64,256]{3,2,1,0:T(8,128)(2,1)S(1)}, bf16[4,1,64,256]{3,2,1,0:T(8,128)(2,1)S(1)}, u32[]{:S(2)}, u32[]{:S(2)}) collective-permute-start(bf16[4,1,64,256]{3,2,1,0:T(8,128)(2,1)S(1)} %get-tuple-element.213), channel_id=1, source_target_pairs={{1,0},{4,1},{5,4},{8,5},{9,8},{12,9},{13,12},{3,2},{6,3},{7,6},{10... | collective-permute-start | bytes 393224 | tf_op jit(solution)/shard_map/ppermute | solution.py:15
  90.0 6.9 %collective-permute-start.9 = (bf16[4,1,64,256]{3,2,1,0:T(8,128)(2,1)}, bf16[4,1,64,256]{3,2,1,0:T(8,128)(2,1)}, u32[]{:S(2)}, u32[]{:S(2)}) collective-permute-start(bf16[4,1,64,256]{3,2,1,0:T(8,128)(2,1)} %get-tuple-element.210), channel_id=1, source_target_pairs={{0,1},{1,4},{4,5},{5,8},{8,9},{9,12},{12,13},{2,3},{3,6},{6,7},{7,... | collective-permute-start | bytes 393224 | tf_op jit(solution)/shard_map/ppermute | solution.py:14
  93.6 3.5 %collective-permute-start.10 = (bf16[4,1,64,256]{3,2,1,0:T(8,128)(2,1)S(1)}, bf16[4,1,64,256]{3,2,1,0:T(8,128)(2,1)}, u32[]{:S(2)}, u32[]{:S(2)}) collective-permute-start(bf16[4,1,64,256]{3,2,1,0:T(8,128)(2,1)S(1)} %get-tuple-element.211), channel_id=1, source_target_pairs={{1,0},{4,1},{5,4},{8,5},{9,8},{12,9},{13,12},{3,2},{6,3},{7,6},{10... | collective-permute-start | bytes 393224 | tf_op jit(solution)/shard_map/ppermute | solution.py:15
  110.4 7.4 %collective-permute-start.11 = (bf16[4,1,64,256]{3,2,1,0:T(8,128)(2,1)}, bf16[4,1,64,256]{3,2,1,0:T(8,128)(2,1)}, u32[]{:S(2)}, u32[]{:S(2)}) collective-permute-start(bf16[4,1,64,256]{3,2,1,0:T(8,128)(2,1)} %get-tuple-element.208), channel_id=1, source_target_pairs={{0,1},{1,4},{4,5},{5,8},{8,9},{9,12},{12,13},{2,3},{3,6},{6,7},{7,... | collective-permute-start | bytes 393224 | tf_op jit(solution)/shard_map/ppermute | solution.py:14
  116.5 3.4 %collective-permute-start.12 = (bf16[4,1,64,256]{3,2,1,0:T(8,128)(2,1)S(1)}, bf16[4,1,64,256]{3,2,1,0:T(8,128)(2,1)}, u32[]{:S(2)}, u32[]{:S(2)}) collective-permute-start(bf16[4,1,64,256]{3,2,1,0:T(8,128)(2,1)S(1)} %get-tuple-element.209), channel_id=1, source_target_pairs={{1,0},{4,1},{5,4},{8,5},{9,8},{12,9},{13,12},{3,2},{6,3},{7,6},{10... | collective-permute-start | bytes 393224 | tf_op jit(solution)/shard_map/ppermute | solution.py:15
  131.5 4.6 %collective-permute-start.15 = (bf16[256,512]{1,0:T(8,128)(2,1)S(1)}, bf16[256,512]{1,0:T(8,128)(2,1)}, u32[]{:S(2)}, u32[]{:S(2)}) collective-permute-start(bf16[256,512]{1,0:T(8,128)(2,1)S(1)} %dynamic-slice_bitcast_fusion.4), channel_id=1, source_target_pairs={{0,1},{1,0},{2,3},{3,2},{4,5},{5,4},{6,7},{7,6},{8,9},{9,8},{10,11... | collective-permute-start | bytes 786440 | tf_op jit(solution)/shard_map/ppermute | solution.py:247
  134.1 5.7 %collective-permute-start.14 = (bf16[2304,128]{0,1:T(8,128)(2,1)S(1)}, bf16[2304,128]{0,1:T(8,128)(2,1)S(1)}, u32[]{:S(2)}, u32[]{:S(2)}) collective-permute-start(bf16[2304,128]{0,1:T(8,128)(2,1)S(1)} %dynamic-slice_bitcast_fusion), channel_id=1, source_target_pairs={{0,1},{1,0},{2,3},{3,2},{4,5},{5,4},{6,7},{7,6},{8,9},{9,8},{10,11... | collective-permute-start | bytes 1769480 | tf_op jit(solution)/shard_map/ppermute | solution.py:247
  136.0 1.9 collective-permute-start.13
  141.0 1.3 collective-permute-start.16
  (30 other events, 156.3 us)
Sparse Core Ops, SparseCore 0:
  18.7 10.5 all-gather.3
  36.0 12.1 all-gather.5
  49.8 10.2 all-gather.7
  141.1 53.3 all-reduce.8
where the time goes:
time: 207 us; the launch traced here: 206 us
  waiting for transfers between devices  66.8 us (32%)
  local copies, waits for them, and re-layouts  34.6 us (17%)
  starting transfers between devices  34.1 us (16%)
  matrix products  26.1 us (13%)
  other arithmetic  19 us (9%)
  between operations  14.3 us (7%)
  blocking collectives  10.8 us (5%)
    psum x1, waiting for transfers between devices, local(): totals.append(lax.psum(pair_sum, 'tiles'))  40.9 us
    ppermute x5, waiting for transfers between devices, gather_blocks(): lax.ppermute(half, 'sections', [(i, (i + k) % chain) for i in range(chain)])  19.9 us
    ppermute x4, starting transfers between devices, halo_rows(): low = lax.ppermute(block[:, -1:], ROW_AXES, forward)  16.4 us
    unnamed x67, local copies, waits for them, and re-layouts  15.2 us
    psum x1, blocking collectives, local(): totals.append(lax.psum(pair_sum, 'tiles'))  10.8 us
    ppermute x5, starting transfers between devices, gather_blocks(): lax.ppermute(half, 'sections', [(i, (i + k) % chain) for i in range(chain)])  8.39 us
    dynamic_slice x3, local copies, waits for them, and re-layouts, gather_blocks(): lax.dynamic_index_in_dim(stacked, (position - b + chain) % chain, 0, keep...  6.9 us
    dot_general x2, matrix products, local(): jnp.dot(grid_taps(hidden_ext, height, breadth, False), spatial_all[b].res...  5.29 us
  transfers between devices with their start and end apart: 21, of which 8 were waited for; matrix products, arithmetic and copies ran while one was open for 16% of the time, Pallas kernels for 0%

commit v1 on v0

--- a/solution.py
+++ b/solution.py
@@ -246,7 +246,7 @@
         theirs = lax.dynamic_index_in_dim(piece, 1 - chan_index, 0, keepdims=False)
         arrived = lax.ppermute(theirs, "chan", [(0, 1), (1, 0)])
         pair_sum = (mine.astype(jnp.float32) + arrived.astype(jnp.float32)).astype(jnp.bfloat16)
-        totals.append(lax.psum(pair_sum, "tiles"))
+        totals.append(jnp.sum(lax.all_gather(pair_sum, "tiles"), axis=0))
     half_inner = inner_width // 2
     grad_reduce = totals[0][None]
     grad_spatial = totals[1].reshape(3, 3, inner_width, half_inner)[None]

time: 207 us -> 261 us (1.26)
  waiting for transfers between devices: 66.8 us -> 116 us
  other arithmetic: 19 us -> 25.5 us
    all_gather x0 -> x3, waiting for transfers between devices: none -> 86.5 us  [local(): totals.append(jnp.sum(lax.all_gather(pair_sum, 'tiles'), axis=0))]
    psum x1 -> x0, waiting for transfers between devices: 40.9 us -> none  [local(): totals.append(lax.psum(pair_sum, 'tiles'))]
    psum x1 -> x0, blocking collectives: 10.8 us -> none  [local(): totals.append(lax.psum(pair_sum, 'tiles'))]
    all_gather x0 -> x1, blocking collectives: none -> 9.9 us  [local(): totals.append(jnp.sum(lax.all_gather(pair_sum, 'tiles'), axis=0))]
    reduce_sum x0 -> x4, other arithmetic: none -> 7.59 us  [local(): totals.append(jnp.sum(lax.all_gather(pair_sum, 'tiles'), axis=0))]
    unnamed x67 -> x58, local copies, waits for them, and re-layouts: 15.2 us -> 9.97 us
    ppermute x4, waiting for transfers between devices: 0.83 us -> 4.77 us  [local(): arrived = lax.ppermute(theirs, 'chan', [(0, 1), (1, 0)])]
    broadcast_in_dim x2 -> x0, other arithmetic: 3.52 us -> none  [the longest x1 1.79 us: local(): grad_reduce = totals[0][None]]
  transfers between devices with their start and end apart: 21 -> 23, of which waited for: 8 -> 13; matrix products, arithmetic and copies ran while one was open for 16% -> 14% of each run, Pallas kernels for 0% -> 0%
where the time goes in v1:
time: 261 us; the launch traced here: 260 us
  waiting for transfers between devices  116 us (44%)
  starting transfers between devices  33.9 us (13%)
  local copies, waits for them, and re-layouts  33.2 us (13%)
  other arithmetic  25.5 us (10%)
  matrix products  25.3 us (10%)
  between operations  14.7 us (6%)
  blocking collectives  9.9 us (4%)
    all_gather x3, waiting for transfers between devices, local(): totals.append(jnp.sum(lax.all_gather(pair_sum, 'tiles'), axis=0))  86.5 us
    ppermute x5, waiting for transfers between devices, gather_blocks(): lax.ppermute(half, 'sections', [(i, (i + k) % chain) for i in range(chain)])  19.9 us
    ppermute x4, starting transfers between devices, halo_rows(): low = lax.ppermute(block[:, -1:], ROW_AXES, forward)  16.4 us
    unnamed x58, local copies, waits for them, and re-layouts  9.97 us
    all_gather x1, blocking collectives, local(): totals.append(jnp.sum(lax.all_gather(pair_sum, 'tiles'), axis=0))  9.9 us
    ppermute x5, starting transfers between devices, gather_blocks(): lax.ppermute(half, 'sections', [(i, (i + k) % chain) for i in range(chain)])  8.39 us
    dynamic_slice x3, local copies, waits for them, and re-layouts, gather_blocks(): lax.dynamic_index_in_dim(stacked, (position - b + chain) % chain, 0, keep...  8.21 us
    reduce_sum x4, other arithmetic, local(): totals.append(jnp.sum(lax.all_gather(pair_sum, 'tiles'), axis=0))  7.59 us
  transfers between devices with their start and end apart: 23, of which 13 were waited for; matrix products, arithmetic and copies ran while one was open for 14% of the time, Pallas kernels for 0%

profile of v1, /device:TPU:0, one launch (start us, length us, event | category | flops | bytes accessed | tf_op | source)
XLA Modules:
  0.0 259.5 jit_solution(10354121529037152638)
XLA Ops:
  7.2 3.0 %collective-permute-start.1 = (bf16[512,256]{1,0:T(8,128)(2,1)}, bf16[512,256]{1,0:T(8,128)(2,1)S(1)}, u32[]{:S(2)}, u32[]{:S(2)}) collective-permute-start(bf16[512,256]{1,0:T(8,128)(2,1)} %bitcast.265), channel_id=1, source_target_pairs={{0,2},{2,0},{1,3},{3,1},{4,6},{6,4},{5,7},{7,5},{8,10},{10,8},{9,1... | collective-permute-start | bytes 786440 | tf_op jit(solution)/shard_map/ppermute | solution.py:39
  10.3 6.5 %collective-permute-done.1 = bf16[512,256]{1,0:T(8,128)(2,1)S(1)} collective-permute-done((bf16[512,256]{1,0:T(8,128)(2,1)}, bf16[512,256]{1,0:T(8,128)(2,1)S(1)}, u32[]{:S(2)}, u32[]{:S(2)}) %collective-permute-start.1) | collective-permute-done | bytes 262176 | tf_op jit(solution)/shard_map/ppermute | solution.py:39
  22.0 12.8 %collective-permute-done.5 = bf16[3,3,256,128]{2,3,1,0:T(8,128)(2,1)S(1)} collective-permute-done((bf16[3,3,256,128]{2,3,1,0:T(8,128)(2,1)S(1)}, bf16[3,3,256,128]{2,3,1,0:T(8,128)(2,1)S(1)}, u32[]{:S(2)}, u32[]{:S(2)}) %collective-permute-start.5) | collective-permute-done | bytes 589856 | tf_op jit(solution)/shard_map/ppermute | solution.py:39
  47.4 2.8 %collective-permute-done.4 = bf16[4,1,64,256]{3,2,1,0:T(8,128)(2,1)S(1)} collective-permute-done((bf16[4,1,64,256]{3,2,1,0:T(8,128)(2,1)S(1)}, bf16[4,1,64,256]{3,2,1,0:T(8,128)(2,1)S(1)}, u32[]{:S(2)}, u32[]{:S(2)}) %collective-permute-start.4) | collective-permute-done | bytes 131104 | tf_op jit(solution)/shard_map/ppermute | solution.py:15
  57.3 3.3 %constant_dynamic-slice_fusion.6 = (bf16[1,3,3,256,256]{3,4,2,1,0:T(8,128)(2,1)}, bf16[1,3,3,256,256]{3,4,2,1,0:T(8,128)(2,1)}) fusion(bf16[2,3,3,256,256]{3,4,2,1,0:T(8,128)(2,1)} %all-gather.14.cloned.1.call-done, s32[]{:T(128)S(6)} %select_n.84, s32[]{:T(128)S(6)} %select_n.82), kind=kLoop, calls=%fused_computation.183 | loop fusion | bytes 4718600 | tf_op jit(solution)/shard_map/jit(dynamic_index_in_dim)/dynamic_slice | solution.py:46
  63.1 3.6 %maximum_convert_fusion.2 = (bf16[4,2,64,256]{3,2,1,0:T(8,128)(2,1)}, f32[4,2,64,256]{3,2,1,0:T(8,128)S(1)}, f32[4,2,64,256]{3,2,1,0:T(8,128)}) fusion(f32[256]{0:T(256)S(1)} %bitcast.271, f32[256]{0:T(256)S(1)} %bitcast.272, bf16[4,2,64,2304]{3,2,1,0:T(8,128)(2,1)} %fusion.50, bf16[2304,256,1,1]{1,0,3,2:T(8,128)(2,1)} %bitcast.250), kind=kOutput, calls=%fused_computation.127 | convolution fusion | flops 604504064 | bytes 4851712 | tf_op jit(solution)/shard_map/dot_general | solution.py:118
  70.2 5.3 %collective-permute-start.7 = (bf16[4,1,64,256]{3,2,1,0:T(8,128)(2,1)S(1)}, bf16[4,1,64,256]{3,2,1,0:T(8,128)(2,1)S(1)}, u32[]{:S(2)}, u32[]{:S(2)}) collective-permute-start(bf16[4,1,64,256]{3,2,1,0:T(8,128)(2,1)S(1)} %get-tuple-element.214), channel_id=1, source_target_pairs={{0,1},{1,4},{4,5},{5,8},{8,9},{9,12},{12,13},{2,3},{3,6},{6,7},{7,... | collective-permute-start | bytes 393224 | tf_op jit(solution)/shard_map/ppermute | solution.py:14
  87.0 3.7 %conditional.6 = (bf16[4,2,64,1024]{3,2,1,0:T(8,128)(2,1)}, f32[4,2,64,256]{3,2,1,0:T(8,128)}, bf16[4,2,64,256]{3,2,1,0:T(8,128)(2,1)S(1)}) conditional(s32[]{:T(128)} %convert_element_type.159, () %tuple.57, (bf16[4,2,64,1024]{3,2,1,0:T(8,128)(2,1)S(1)}, bf16[4,2,64,1024]{3,2,1,0:T(8,128)(2,1)S(1)}, f32[4,2,64,256]{3,2,1,0:T(8,128)S(1)}, ...), branch_computations={%region_0.1_spmd, %region_1.2_spmd} | conditional | flops 270008320 | bytes 6032408 | solution.py:192
  88.2 2.5 multiply_convert_fusion
  91.4 3.7 %collective-permute-start.9 = (bf16[4,1,64,256]{3,2,1,0:T(8,128)(2,1)}, bf16[4,1,64,256]{3,2,1,0:T(8,128)(2,1)}, u32[]{:S(2)}, u32[]{:S(2)}) collective-permute-start(bf16[4,1,64,256]{3,2,1,0:T(8,128)(2,1)} %get-tuple-element.212), channel_id=1, source_target_pairs={{0,1},{1,4},{4,5},{5,8},{8,9},{9,12},{12,13},{2,3},{3,6},{6,7},{7,... | collective-permute-start | bytes 393224 | tf_op jit(solution)/shard_map/ppermute | solution.py:14
  99.5 3.1 %conditional.7 = (f32[4,2,64,256]{3,2,1,0:T(8,128)}, bf16[4,2,64,256]{3,2,1,0:T(8,128)(2,1)S(1)}) conditional(s32[]{:T(128)} %convert_element_type.159, () %tuple.59, (f32[4,2,64,256]{3,2,1,0:T(8,128)}, bf16[4,4,64,256]{3,2,1,0:T(8,128)(2,1)S(1)}, bf16[1,3,3,256,256]{3,4,2,1,0:T(8,128)(2,1)}, f32[2,256]{1,0:T(2,128)S(1)}) %tuple.141), branch_computations={%region_2.3_spmd, %region_3.4_spmd} | conditional | flops 604504064 | bytes 17960008 | solution.py:208
  103.3 2.8 %conditional.8 = (bf16[4,2,64,1024]{3,2,1,0:T(8,128)(2,1)}) conditional(s32[]{:T(128)} %convert_element_type.158, () %tuple.56, (bf16[4,2,64,1024]{3,2,1,0:T(8,128)(2,1)}, bf16[4,2,64,256]{3,2,1,0:T(8,128)(2,1)S(1)}, bf16[1024,256]{1,0:T(8,128)(2,1)}) %tuple.61), branch_computations={%region_4.5_spmd, %region_5.6_spmd} | conditional | flops 270008320 | bytes 2883592 | solution.py:233
  103.3 2.8 %add_convert_fusion = bf16[4,2,64,1024]{3,2,1,0:T(8,128)(2,1)} fusion(bf16[4,2,64,1024]{3,2,1,0:T(8,128)(2,1)} %get-tuple-element.96, bf16[4,2,64,256]{3,2,1,0:T(8,128)(2,1)S(1)} %get-tuple-element.97, bf16[1024,256]{1,0:T(8,128)(2,1)} %get-tuple-element.98), kind=kOutput, calls=%fused_computation.21 | convolution fusion | flops 270008320 | bytes 2883584 | tf_op jit(solution)/shard_map/cond/branch_1_fun/dot_general | solution.py:226
  106.2 4.2 %conditional.9 = (bf16[4,2,64,1024]{3,2,1,0:T(8,128)(2,1)}, f32[4,2,64,256]{3,2,1,0:T(8,128)S(1)}, bf16[4,2,64,256]{3,2,1,0:T(8,128)(2,1)S(1)}) conditional(s32[]{:T(128)} %convert_element_type.152, () %tuple.55, (bf16[4,2,64,1024]{3,2,1,0:T(8,128)(2,1)S(1)}, bf16[4,2,64,1024]{3,2,1,0:T(8,128)(2,1)}, f32[4,2,64,256]{3,2,1,0:T(8,128)}, ...), branch_computations={%region_6.7_spmd, %region_7.8_spmd} | conditional | flops 270008320 | bytes 10226768 | solution.py:192
  106.2 2.5 compare_select_fusion.1
  111.8 6.1 %collective-permute-start.11 = (bf16[4,1,64,256]{3,2,1,0:T(8,128)(2,1)}, bf16[4,1,64,256]{3,2,1,0:T(8,128)(2,1)}, u32[]{:S(2)}, u32[]{:S(2)}) collective-permute-start(bf16[4,1,64,256]{3,2,1,0:T(8,128)(2,1)} %get-tuple-element.210), channel_id=1, source_target_pairs={{0,1},{1,4},{4,5},{5,8},{8,9},{9,12},{12,13},{2,3},{3,6},{6,7},{7,... | collective-permute-start | bytes 393224 | tf_op jit(solution)/shard_map/ppermute | solution.py:14
  122.4 2.5 conditional.10
  124.9 7.3 %conditional.11 = (bf16[2,512,256]{2,1,0:T(8,128)(2,1)S(1)}, bf16[2,2304,128]{1,2,0:T(8,128)(2,1)S(1)}, bf16[2,4,128]{2,0,1:T(2,128)(2,1)S(1)}, bf16[2,256,512]{2,1,0:T(8,128)(2,1)S(1)}, bf16[2,4,128]{2,1,0:T(4,128)(2,1)S(1)}) conditional(s32[]{:T(128)} %clamp.3, (bf16[4,2,64,1024]{3,2,1,0:T(8,128)(2,1)}, bf16[4,2,64,256]{3,2,1,0:T(8,128)(2,1)S(1)}, ...), branch_computations={%region_10.15_spmd, %region_15.20_spmd} | conditional | flops 1142753280 | bytes 25323728 | solution.py:236
  143.5 9.9 %all-gather.4 = bf16[4,4,128]{2,1,0:T(4,128)(2,1)S(1)} all-gather(bf16[1,4,128]{2,1,0:T(4,128)(2,1)S(1)} %fusion.72), channel_id=5, replica_groups=mesh['groups'=2,'tiles'=4,'sections'=2,'chan'=2] {'tiles'}, dimensions={0}, use_global_device_ids=true | all-gather | bytes 5120 | tf_op jit(solution)/shard_map/all_gather | solution.py:249
  154.0 10.1 %all-gather.22.cloned.1.call-done = bf16[1024,512]{1,0:T(8,128)(2,1)} async-done(((bf16[256,512]{1,0:T(8,128)(2,1)}), bf16[1024,512]{1,0:T(8,128)(2,1)}) %all-gather.22.cloned.1.call-update) | async-done | bytes 1048592 | tf_op jit(solution)/shard_map/all_gather | solution.py:249
  166.3 27.2 %all-gather.18.cloned.1.call-done = bf16[2048,256]{1,0:T(8,128)(2,1)} async-done(((bf16[512,256]{1,0:T(8,128)(2,1)}), bf16[2048,256]{1,0:T(8,128)(2,1)}) %all-gather.18.cloned.1.call-update) | async-done | bytes 1048592 | tf_op jit(solution)/shard_map/all_gather | solution.py:249
  195.6 49.2 %all-gather.20.cloned.1.call-done = bf16[9216,128]{0,1:T(8,128)(2,1)} async-done(((bf16[2304,128]{0,1:T(8,128)(2,1)}), bf16[9216,128]{0,1:T(8,128)(2,1)}) %all-gather.20.cloned.1.call-update) | async-done | bytes 2359312 | tf_op jit(solution)/shard_map/all_gather | solution.py:249
  244.8 3.5 %reshape.174 = bf16[4,2304,128]{1,0,2:T(4,128)(2,1)S(1)} reshape(bf16[9216,128]{0,1:T(8,128)(2,1)} %all-gather.20.cloned.1.call-done) | data formatting | bytes 4718592 | tf_op jit(solution)/shard_map/all_gather | solution.py:249
  248.4 3.3 %reduce_sum.121 = bf16[2304,128]{0,1:T(8,128)(2,1)S(1)} reduce(bf16[4,2304,128]{1,0,2:T(4,128)(2,1)S(1)} %reshape.174, bf16[]{:T(256)} %constant.159.clone.1), dimensions={0}, to_apply=%region_21.22 | reduce | flops 884736 | bytes 2949122 | tf_op jit(solution)/shard_map/reduce_sum | solution.py:249
  (210 shorter events, 86.1 us)
Async XLA Ops:
  7.2 32.5 %copy-start = (bf16[2,1024]{1,0:T(2,128)(2,1)S(1)}, bf16[2,1024]{1,0:T(2,128)(2,1)}, u32[]{:S(2)}) copy-start(bf16[2,1024]{1,0:T(2,128)(2,1)} %param.24) | copy-start | bytes 12292
  7.2 34.0 %all-gather.12.cloned.1.call-start = ((), (), s32[]{:S(2)}) async-start(), calls=%async_computation | async-start | bytes 1572864 | tf_op jit(solution)/shard_map/all_gather | solution.py:44
  7.2 9.5 %collective-permute-start.1 = (bf16[512,256]{1,0:T(8,128)(2,1)}, bf16[512,256]{1,0:T(8,128)(2,1)S(1)}, u32[]{:S(2)}, u32[]{:S(2)}) collective-permute-start(bf16[512,256]{1,0:T(8,128)(2,1)} %bitcast.265), channel_id=1, source_target_pairs={{0,2},{2,0},{1,3},{3,1},{4,6},{6,4},{5,7},{7,5},{8,10},{10,8},{9,1... | collective-permute-start | bytes 786440 | tf_op jit(solution)/shard_map/ppermute | solution.py:39
  18.7 38.7 %all-gather.14.cloned.1.call-start = ((), (), s32[]{:S(2)}) async-start(), calls=%async_computation.1 | async-start | bytes 3538944 | tf_op jit(solution)/shard_map/all_gather | solution.py:44
  20.2 14.6 %collective-permute-start.5 = (bf16[3,3,256,128]{2,3,1,0:T(8,128)(2,1)S(1)}, bf16[3,3,256,128]{2,3,1,0:T(8,128)(2,1)S(1)}, u32[]{:S(2)}, u32[]{:S(2)}) collective-permute-start(bf16[3,3,256,128]{2,3,1,0:T(8,128)(2,1)S(1)} %bitcast.251), channel_id=1, source_target_pairs={{0,2},{2,0},{1,3},{3,1},{4,6},{6,4},{5,7},{7,5},{8,10},{10,8},{9,1... | collective-permute-start | bytes 1769480 | tf_op jit(solution)/shard_map/ppermute | solution.py:39
  35.9 30.8 %all-gather.16.cloned.1.call-start = ((), (), s32[]{:S(2)}) async-start(), calls=%async_computation.2 | async-start | bytes 1572864 | tf_op jit(solution)/shard_map/all_gather | solution.py:44
  36.0 4.5 %collective-permute-start.2 = (f32[2,256]{1,0:T(2,128)S(1)}, f32[2,256]{1,0:T(2,128)S(1)}, u32[]{:S(2)}, u32[]{:S(2)}) collective-permute-start(f32[2,256]{1,0:T(2,128)S(1)} %bitcast.292), channel_id=1, source_target_pairs={{0,2},{2,0},{1,3},{3,1},{4,6},{6,4},{5,7},{7,5},{8,10},{10,8},{9,1... | collective-permute-start | bytes 6152 | tf_op jit(solution)/shard_map/ppermute | solution.py:39
  37.5 3.6 %collective-permute-start = (f32[2,256]{1,0:T(2,128)S(1)}, f32[2,256]{1,0:T(2,128)S(1)}, u32[]{:S(2)}, u32[]{:S(2)}) collective-permute-start(f32[2,256]{1,0:T(2,128)S(1)} %bitcast.291), channel_id=1, source_target_pairs={{0,2},{2,0},{1,3},{3,1},{4,6},{6,4},{5,7},{7,5},{8,10},{10,8},{9,1... | collective-permute-start | bytes 6152 | tf_op jit(solution)/shard_map/ppermute | solution.py:39
  38.1 8.4 %collective-permute-start.6 = (bf16[256,512]{1,0:T(8,128)(2,1)S(1)}, bf16[256,512]{1,0:T(8,128)(2,1)S(1)}, u32[]{:S(2)}, u32[]{:S(2)}) collective-permute-start(bf16[256,512]{1,0:T(8,128)(2,1)S(1)} %bitcast.266), channel_id=1, source_target_pairs={{0,2},{2,0},{1,3},{3,1},{4,6},{6,4},{5,7},{7,5},{8,10},{10,8},{9,1... | collective-permute-start | bytes 786440 | tf_op jit(solution)/shard_map/ppermute | solution.py:39
  43.8 3.6 %collective-permute-start.3 = (bf16[4,1,64,256]{3,2,1,0:T(8,128)(2,1)S(1)}, bf16[4,1,64,256]{3,2,1,0:T(8,128)(2,1)S(1)}, u32[]{:S(2)}, u32[]{:S(2)}) collective-permute-start(bf16[4,1,64,256]{3,2,1,0:T(8,128)(2,1)S(1)} %get-tuple-element.216), channel_id=1, source_target_pairs={{0,1},{1,4},{4,5},{5,8},{8,9},{9,12},{12,13},{2,3},{3,6},{6,7},{7,... | collective-permute-start | bytes 393224 | tf_op jit(solution)/shard_map/ppermute | solution.py:14
  45.2 5.0 %collective-permute-start.4 = (bf16[4,1,64,256]{3,2,1,0:T(8,128)(2,1)S(1)}, bf16[4,1,64,256]{3,2,1,0:T(8,128)(2,1)S(1)}, u32[]{:S(2)}, u32[]{:S(2)}) collective-permute-start(bf16[4,1,64,256]{3,2,1,0:T(8,128)(2,1)S(1)} %get-tuple-element.217), channel_id=1, source_target_pairs={{1,0},{4,1},{5,4},{8,5},{9,8},{12,9},{13,12},{3,2},{6,3},{7,6},{10... | collective-permute-start | bytes 393224 | tf_op jit(solution)/shard_map/ppermute | solution.py:15
  47.4 116.8 %all-gather.22.cloned.1.call-start = ((), (), s32[]{:S(2)}) async-start(), calls=%async_computation.5 | async-start | bytes 1310720 | tf_op jit(solution)/shard_map/all_gather | solution.py:249
  70.2 10.2 %collective-permute-start.7 = (bf16[4,1,64,256]{3,2,1,0:T(8,128)(2,1)S(1)}, bf16[4,1,64,256]{3,2,1,0:T(8,128)(2,1)S(1)}, u32[]{:S(2)}, u32[]{:S(2)}) collective-permute-start(bf16[4,1,64,256]{3,2,1,0:T(8,128)(2,1)S(1)} %get-tuple-element.214), channel_id=1, source_target_pairs={{0,1},{1,4},{4,5},{5,8},{8,9},{9,12},{12,13},{2,3},{3,6},{6,7},{7,... | collective-permute-start | bytes 393224 | tf_op jit(solution)/shard_map/ppermute | solution.py:14
  75.5 5.5 %collective-permute-start.8 = (bf16[4,1,64,256]{3,2,1,0:T(8,128)(2,1)S(1)}, bf16[4,1,64,256]{3,2,1,0:T(8,128)(2,1)S(1)}, u32[]{:S(2)}, u32[]{:S(2)}) collective-permute-start(bf16[4,1,64,256]{3,2,1,0:T(8,128)(2,1)S(1)} %get-tuple-element.215), channel_id=1, source_target_pairs={{1,0},{4,1},{5,4},{8,5},{9,8},{12,9},{13,12},{3,2},{6,3},{7,6},{10... | collective-permute-start | bytes 393224 | tf_op jit(solution)/shard_map/ppermute | solution.py:15
  91.4 6.8 %collective-permute-start.9 = (bf16[4,1,64,256]{3,2,1,0:T(8,128)(2,1)}, bf16[4,1,64,256]{3,2,1,0:T(8,128)(2,1)}, u32[]{:S(2)}, u32[]{:S(2)}) collective-permute-start(bf16[4,1,64,256]{3,2,1,0:T(8,128)(2,1)} %get-tuple-element.212), channel_id=1, source_target_pairs={{0,1},{1,4},{4,5},{5,8},{8,9},{9,12},{12,13},{2,3},{3,6},{6,7},{7,... | collective-permute-start | bytes 393224 | tf_op jit(solution)/shard_map/ppermute | solution.py:14
  95.0 3.5 %collective-permute-start.10 = (bf16[4,1,64,256]{3,2,1,0:T(8,128)(2,1)S(1)}, bf16[4,1,64,256]{3,2,1,0:T(8,128)(2,1)}, u32[]{:S(2)}, u32[]{:S(2)}) collective-permute-start(bf16[4,1,64,256]{3,2,1,0:T(8,128)(2,1)S(1)} %get-tuple-element.213), channel_id=1, source_target_pairs={{1,0},{4,1},{5,4},{8,5},{9,8},{12,9},{13,12},{3,2},{6,3},{7,6},{10... | collective-permute-start | bytes 393224 | tf_op jit(solution)/shard_map/ppermute | solution.py:15
  111.8 7.4 %collective-permute-start.11 = (bf16[4,1,64,256]{3,2,1,0:T(8,128)(2,1)}, bf16[4,1,64,256]{3,2,1,0:T(8,128)(2,1)}, u32[]{:S(2)}, u32[]{:S(2)}) collective-permute-start(bf16[4,1,64,256]{3,2,1,0:T(8,128)(2,1)} %get-tuple-element.210), channel_id=1, source_target_pairs={{0,1},{1,4},{4,5},{5,8},{8,9},{9,12},{12,13},{2,3},{3,6},{6,7},{7,... | collective-permute-start | bytes 393224 | tf_op jit(solution)/shard_map/ppermute | solution.py:14
  117.9 3.4 %collective-permute-start.12 = (bf16[4,1,64,256]{3,2,1,0:T(8,128)(2,1)S(1)}, bf16[4,1,64,256]{3,2,1,0:T(8,128)(2,1)}, u32[]{:S(2)}, u32[]{:S(2)}) collective-permute-start(bf16[4,1,64,256]{3,2,1,0:T(8,128)(2,1)S(1)} %get-tuple-element.211), channel_id=1, source_target_pairs={{1,0},{4,1},{5,4},{8,5},{9,8},{12,9},{13,12},{3,2},{6,3},{7,6},{10... | collective-permute-start | bytes 393224 | tf_op jit(solution)/shard_map/ppermute | solution.py:15
  132.2 3.6 %collective-permute-start.15 = (bf16[256,512]{1,0:T(8,128)(2,1)S(1)}, bf16[256,512]{1,0:T(8,128)(2,1)S(1)}, u32[]{:S(2)}, u32[]{:S(2)}) collective-permute-start(bf16[256,512]{1,0:T(8,128)(2,1)S(1)} %dynamic-slice_bitcast_fusion.4), channel_id=1, source_target_pairs={{0,1},{1,0},{2,3},{3,2},{4,5},{5,4},{6,7},{7,6},{8,9},{9,8},{10,11... | collective-permute-start | bytes 786440 | tf_op jit(solution)/shard_map/ppermute | solution.py:247
  136.6 56.9 %all-gather.18.cloned.1.call-start = ((), (), s32[]{:S(2)}) async-start(), calls=%async_computation.3 | async-start | bytes 1310720 | tf_op jit(solution)/shard_map/all_gather | solution.py:249
  136.7 1.6 collective-permute-start.13
  139.1 105.8 %all-gather.20.cloned.1.call-start = ((), (), s32[]{:S(2)}) async-start(), calls=%async_computation.4 | async-start | bytes 2949120 | tf_op jit(solution)/shard_map/all_gather | solution.py:249
  139.2 2.1 collective-permute-start.14
  142.2 1.3 collective-permute-start.16
  (29 other events, 191.2 us)
Sparse Core Ops, SparseCore 0:
  18.7 10.5 all-gather.11
  36.0 12.1 all-gather.13
  49.8 10.2 all-gather.15
  136.7 27.3 all-gather.21
  166.1 27.2 all-gather.17
  195.4 49.3 all-gather.19
